TPU v7x, 512 devices: a whole 4x8x8 slice. The times are simulated.
512 devices in a mesh: expert: 64 (over z, y), tensor: 8 (over x, core).
Axes of the slice: x: 4, y: 8, z: 8, core: 2. Of those that a mesh axis runs over, the one named last changes fastest.
Arguments:
- hidden_rows: bfloat16 [2, 1024, 3584], P(None, 'expert', 'tensor'), may hold values from -6 to 6
- draft_len: int32 [2, 256], P(None, 'expert'), may hold values from 1 to 4, 640 in all within a row
- expert_ids: int32 [2, 1024, 8], P(None, 'expert'), may hold values from 0 to 55, all different within a row; in each aligned block of 16 rows (0 to 15, 16 to 31, ..., all dimensions but the last counted through in order) at most 4 rows name the same one
- replica: int32 [2, 1024, 8], P(None, 'expert'), may hold values from 0 to 1
- route_gain: float32 [2, 1024, 8], P(None, 'expert'), may hold values from 0.03 to 0.5
- slot_up: bfloat16 [64, 3584, 1024], P('expert', None, 'tensor'), may hold values from -0.09375 to 0.09375
- slot_down: bfloat16 [64, 1024, 3584], P('expert', 'tensor'), may hold values from -0.1875 to 0.1875
- shared_up: bfloat16 [3584, 1024], P(None, 'tensor'), may hold values from -0.09375 to 0.09375
- shared_down: bfloat16 [1024, 3584], P('tensor'), may hold values from -0.1875 to 0.1875
Outputs:
- mixed: bfloat16 [2, 1024, 3584], P(None, 'expert', 'tensor')
Inputs may be any that keep to these rules, and one draw needn't show every extreme that they name: `expert_ids`: in each step, the 16 row places of one index of expert (live or not) name any one expert at most 4 times. Only the first 8 experts have a replica slot; for the other experts the value has no effect. `draft_len`: in each step the lengths of all 256 requests sum to 640.
All inputs are finite; a program needn't handle non-finite values. No bound on the sum of `draft_len` on one device may be relied on, other than what follows from the above.
Results may differ from a plain program's by a relative error of at most 0.019.
Values may be sent and summed in bfloat16 or wider, within the bound.
No kernel may reach another device: no remote copies, remote signals or barrier semaphores. Data moves between devices by JAX's collectives and lax.ppermute only.
A program may use at most 192 MiB of HBM per device.

v0:
```python
import jax
import jax.numpy as jnp
from jax import lax
from jax.sharding import PartitionSpec as P


def route_plan(lengths, chosen, second, gains, slot_count, capacity):
    row_count, top_count = chosen.shape
    span_rows = row_count // lengths.shape[0]
    positions = jnp.arange(row_count, dtype=jnp.int32)
    limit = jnp.repeat(lengths, span_rows, total_repeat_length=row_count)
    live_mask = positions % span_rows < limit
    replicas = slot_count // 8
    experts_all = slot_count - replicas
    slot_index = jnp.where(
        (chosen < replicas) & (second == 1), chosen + experts_all, chosen
    ).reshape(-1)
    valid = jnp.broadcast_to(live_mask[:, None], chosen.shape).reshape(-1)
    onehot = (
        (slot_index[:, None] == jnp.arange(slot_count, dtype=jnp.int32)[None, :]) & valid[:, None]
    ).astype(jnp.int32)
    earlier = jnp.cumsum(onehot, axis=0) - onehot
    order_rank = jnp.sum(earlier * onehot, axis=1)
    target = jnp.where(valid, slot_index * capacity + order_rank, -1)
    buffer_ids = jnp.arange(slot_count * capacity, dtype=jnp.int32)
    picker = jnp.any(
        target.reshape(row_count, top_count)[None, :, :] == buffer_ids[:, None, None], axis=2
    ).astype(jnp.bfloat16)
    weights = (gains * live_mask[:, None].astype(jnp.float32)).reshape(-1)
    return (live_mask, target, picker, weights)


def shards(
    hidden_rows,
    draft_len,
    expert_ids,
    replica,
    route_gain,
    slot_up,
    slot_down,
    shared_up,
    shared_down,
):
    slot_count = lax.axis_size("expert")
    step_count, row_count, _ = hidden_rows.shape
    top_count = expert_ids.shape[2]
    capacity = row_count * top_count // (slot_count - slot_count // 8) + 2
    gathered = lax.all_gather(hidden_rows, "tensor", axis=2, tiled=True)
    width_full = gathered.shape[2]
    plans = [
        route_plan(
            draft_len[index],
            expert_ids[index],
            replica[index],
            route_gain[index],
            slot_count,
            capacity,
        )
        for index in range(step_count)
    ]
    outgoing = []
    for index in range(step_count):
        source = gathered[index]
        packed = jnp.dot(plans[index][2], source, preferred_element_type=jnp.float32).astype(
            jnp.bfloat16
        )
        outgoing.append(packed.reshape(slot_count, capacity, source.shape[1]))
    groups = [[index] for index in range(step_count)]
    returned = [None] * step_count
    for step_group in groups:
        batch = jnp.concatenate([outgoing[index] for index in step_group], axis=1)
        received = lax.all_to_all(batch, "expert", split_axis=0, concat_axis=0, tiled=True)
        flat_rows = received.reshape(-1, width_full)
        hidden = jax.nn.silu(
            jnp.dot(flat_rows, slot_up[0], preferred_element_type=jnp.float32)
        ).astype(jnp.bfloat16)
        partial_value = jnp.dot(hidden, slot_down[0], preferred_element_type=jnp.float32).astype(
            jnp.bfloat16
        )
        partial_value = partial_value.reshape(received.shape[0], -1, width_full)
        answer = lax.all_to_all(partial_value, "expert", split_axis=0, concat_axis=0, tiled=True)
        out_width = answer.shape[2]
        for place, index in enumerate(step_group):
            returned[index] = answer.reshape(-1, out_width)
    routed_terms = []
    shared_terms = []
    for index in range(step_count):
        live_mask, target, picker, weights = plans[index]
        fetched = jnp.take(returned[index], jnp.maximum(target, 0), axis=0).astype(jnp.float32)
        routed = jnp.sum(
            (fetched * weights[:, None]).reshape(row_count, top_count, fetched.shape[1]), axis=1
        )
        shared_act = jax.nn.silu(
            jnp.dot(gathered[index], shared_up, preferred_element_type=jnp.float32)
        ).astype(jnp.bfloat16)
        shared_out = jnp.dot(shared_act, shared_down, preferred_element_type=jnp.float32)
        routed_terms.append(routed)
        shared_terms.append(shared_out)
    live_all = jnp.stack([plans[index][0] for index in range(step_count)]).astype(jnp.float32)[
        :, :, None
    ]
    terms = (jnp.stack(routed_terms) + jnp.stack(shared_terms)) * live_all
    summed = lax.psum_scatter(terms.astype(jnp.bfloat16), "tensor", scatter_dimension=2, tiled=True)
    return summed


def solution(mesh):
    return jax.shard_map(
        shards,
        mesh=mesh,
        in_specs=(
            P(None, "expert", "tensor"),
            P(None, "expert"),
            P(None, "expert", None),
            P(None, "expert", None),
            P(None, "expert", None),
            P("expert", None, "tensor"),
            P("expert", "tensor", None),
            P(None, "tensor"),
            P("tensor", None),
        ),
        out_specs=P(None, "expert", "tensor"),
        check_vma=False,
    )
```

profile of v0, /device:TPU:8, one launch (start us, length us, event | category | flops | bytes accessed | tf_op | source)
XLA Modules:
  0.0 314.1 jit_solution(14471994504677403090)
XLA Ops:
  13.0 15.1 %all_gather.3 = bf16[2,16,3584]{1,0,2:T(2,128)(2,1)S(1)} all-gather(bf16[2,16,448]{1,0,2:T(2,128)(2,1)S(1)} %copy.58), channel_id=1, replica_groups=mesh['expert'=64,'tensor'=8] {'tensor'}, dimensions={2}, use_global_device_ids=true | all-gather | bytes 258048 | tf_op jit(solution)/shard_map/all_gather | solution.py:48
  28.1 3.5 %fusion.58 = (bf16[1,16,3584]{1,0,2:T(2,128)(2,1)S(1)}, bf16[1,16,3584]{1,0,2:T(2,128)(2,1)}) fusion(bf16[2,16,3584]{1,0,2:T(2,128)(2,1)S(1)} %all_gather.3), kind=kLoop, calls=%fused_computation.82 | loop fusion | bytes 458752 | tf_op jit(solution)/shard_map/slice | solution.py:63
  35.5 16.6 %all-to-all-start = ((bf16[64,4,3584]{2,1,0:T(4,128)(2,1)}), bf16[64,4,3584]{2,1,0:T(4,128)(2,1)S(1)}, u32[]{:S(2)}, u32[]{:S(2)}) async-start(bf16[64,4,3584]{2,1,0:T(4,128)(2,1)} %reshape.191), calls=%async_computation | async-start | bytes 3670016 | tf_op jit(solution)/shard_map/all_to_all | solution.py:72
  53.2 3.5 %copy.76 = bf16[1,16,3584]{2,1,0:T(8,128)(2,1)S(1)} copy(bf16[1,16,3584]{1,0,2:T(2,128)(2,1)} %get-tuple-element.32) | data formatting | bytes 229376
  56.9 1.9 convolution_convert_fusion.2
  58.8 4.1 %reshape.196 = bf16[64,4,3584]{2,1,0:T(4,128)(2,1)} reshape(bf16[256,3584]{1,0:T(8,128)(2,1)} %convolution_convert_fusion.2) | data formatting | bytes 3670016 | tf_op jit(solution)/shard_map/reshape | solution.py:67
  62.9 36.4 %all-to-all-done = bf16[64,4,3584]{2,1,0:T(4,128)(2,1)S(1)} async-done(((bf16[64,4,3584]{2,1,0:T(4,128)(2,1)}), bf16[64,4,3584]{2,1,0:T(4,128)(2,1)S(1)}, u32[]{:S(2)}, u32[]{:S(2)}) %all-to-all-start) | async-done | bytes 1835040 | tf_op jit(solution)/shard_map/all_to_all | solution.py:72
  99.3 8.4 %all-to-all-start.2 = ((bf16[64,4,3584]{2,1,0:T(4,128)(2,1)}), bf16[64,4,3584]{2,1,0:T(4,128)(2,1)}, u32[]{:S(2)}, u32[]{:S(2)}) async-start(bf16[64,4,3584]{2,1,0:T(4,128)(2,1)} %reshape.196), calls=%async_computation.2 | async-start | bytes 3670016 | tf_op jit(solution)/shard_map/all_to_all | solution.py:72
  109.2 2.9 convolution_convert_fusion.1
  113.6 40.3 %all-to-all-done.2 = bf16[64,4,3584]{2,1,0:T(4,128)(2,1)} async-done(((bf16[64,4,3584]{2,1,0:T(4,128)(2,1)}), bf16[64,4,3584]{2,1,0:T(4,128)(2,1)}, u32[]{:S(2)}, u32[]{:S(2)}) %all-to-all-start.2) | async-done | bytes 1835040 | tf_op jit(solution)/shard_map/all_to_all | solution.py:72
  153.9 7.5 %all-to-all-start.1 = ((bf16[64,4,3584]{2,1,0:T(4,128)(2,1)}), bf16[64,4,3584]{2,1,0:T(4,128)(2,1)S(1)}, u32[]{:S(2)}, u32[]{:S(2)}) async-start(bf16[64,4,3584]{2,1,0:T(4,128)(2,1)} %reshape.193), calls=%async_computation.1 | async-start | bytes 3670016 | tf_op jit(solution)/shard_map/all_to_all | solution.py:81
  161.5 3.9 %reshape.197 = bf16[256,3584]{1,0:T(8,128)(2,1)} reshape(bf16[64,4,3584]{2,1,0:T(4,128)(2,1)} %all-to-all-done.2) | data formatting | bytes 3670016 | tf_op jit(solution)/shard_map/reshape | solution.py:73
  165.4 4.2 %convolution_convert_fusion = bf16[256,3584]{1,0:T(8,128)(2,1)} fusion(bf16[1,128,3584]{2,1,0:T(8,128)(2,1)S(1)} %copy-done, bf16[256,3584]{1,0:T(8,128)(2,1)} %reshape.197, bf16[1,3584,128]{2,1,0:T(8,128)(2,1)} %param.22), kind=kOutput, calls=%fused_computation.4 | convolution fusion | flops 470843392 | bytes 5505024 | tf_op jit(solution)/shard_map/dot_general | solution.py:77
  169.6 4.1 %reshape.198 = bf16[64,4,3584]{2,1,0:T(4,128)(2,1)} reshape(bf16[256,3584]{1,0:T(8,128)(2,1)} %convolution_convert_fusion) | data formatting | bytes 3670016 | tf_op jit(solution)/shard_map/reshape | solution.py:80
  173.6 33.8 %all-to-all-done.1 = bf16[64,4,3584]{2,1,0:T(4,128)(2,1)S(1)} async-done(((bf16[64,4,3584]{2,1,0:T(4,128)(2,1)}), bf16[64,4,3584]{2,1,0:T(4,128)(2,1)S(1)}, u32[]{:S(2)}, u32[]{:S(2)}) %all-to-all-start.1) | async-done | bytes 1835040 | tf_op jit(solution)/shard_map/all_to_all | solution.py:81
  208.7 7.3 %all-to-all-start.3 = ((bf16[64,4,3584]{2,1,0:T(4,128)(2,1)}), bf16[64,4,3584]{2,1,0:T(4,128)(2,1)}, u32[]{:S(2)}, u32[]{:S(2)}) async-start(bf16[64,4,3584]{2,1,0:T(4,128)(2,1)} %reshape.198), calls=%async_computation.3 | async-start | bytes 3670016 | tf_op jit(solution)/shard_map/all_to_all | solution.py:81
  219.2 3.0 reshape.194
  222.2 2.0 gather_fusion.1
  224.2 35.6 %all-to-all-done.3 = bf16[64,4,3584]{2,1,0:T(4,128)(2,1)} async-done(((bf16[64,4,3584]{2,1,0:T(4,128)(2,1)}), bf16[64,4,3584]{2,1,0:T(4,128)(2,1)}, u32[]{:S(2)}, u32[]{:S(2)}) %all-to-all-start.3) | async-done | bytes 1835040 | tf_op jit(solution)/shard_map/all_to_all | solution.py:81
  259.8 2.9 reshape.199
  262.8 2.0 gather_fusion.3
  266.7 1.9 bitcast_reduce_fusion
  268.8 2.4 copy.69
  272.9 32.6 %reduce-scatter.4.cloned.1.call-done = bf16[448,32]{1,0:T(8,128)(2,1)} async-done(((bf16[3584,32]{1,0:T(8,128)(2,1)}), bf16[448,32]{1,0:T(8,128)(2,1)}) %reduce-scatter.4.cloned.1.call-update) | async-done | bytes 28688
  (76 shorter events, 24.3 us)
Async XLA Ops:
  6.5 102.7 %copy-start = (bf16[1,128,3584]{2,1,0:T(8,128)(2,1)S(1)}, bf16[1,128,3584]{2,1,0:T(8,128)(2,1)}, u32[]{:S(2)}) copy-start(bf16[1,128,3584]{2,1,0:T(8,128)(2,1)} %param.23) | copy-start | bytes 2752516
  35.5 63.8 %all-to-all-start = ((bf16[64,4,3584]{2,1,0:T(4,128)(2,1)}), bf16[64,4,3584]{2,1,0:T(4,128)(2,1)S(1)}, u32[]{:S(2)}, u32[]{:S(2)}) async-start(bf16[64,4,3584]{2,1,0:T(4,128)(2,1)} %reshape.191), calls=%async_computation | async-start | bytes 3670016 | tf_op jit(solution)/shard_map/all_to_all | solution.py:72
  99.3 54.6 %all-to-all-start.2 = ((bf16[64,4,3584]{2,1,0:T(4,128)(2,1)}), bf16[64,4,3584]{2,1,0:T(4,128)(2,1)}, u32[]{:S(2)}, u32[]{:S(2)}) async-start(bf16[64,4,3584]{2,1,0:T(4,128)(2,1)} %reshape.196), calls=%async_computation.2 | async-start | bytes 3670016 | tf_op jit(solution)/shard_map/all_to_all | solution.py:72
  153.9 53.5 %all-to-all-start.1 = ((bf16[64,4,3584]{2,1,0:T(4,128)(2,1)}), bf16[64,4,3584]{2,1,0:T(4,128)(2,1)S(1)}, u32[]{:S(2)}, u32[]{:S(2)}) async-start(bf16[64,4,3584]{2,1,0:T(4,128)(2,1)} %reshape.193), calls=%async_computation.1 | async-start | bytes 3670016 | tf_op jit(solution)/shard_map/all_to_all | solution.py:81
  173.6 42.8 %copy-start.4 = (f32[2,16,8]{1,2,0:T(8,128)S(1)}, f32[2,16,8]{1,2,0:T(8,128)}, u32[]{:S(2)}) copy-start(f32[2,16,8]{1,2,0:T(8,128)} %param.21) | copy-start | bytes 3076
  207.4 1.3 copy-start.1
  208.7 51.1 %all-to-all-start.3 = ((bf16[64,4,3584]{2,1,0:T(4,128)(2,1)}), bf16[64,4,3584]{2,1,0:T(4,128)(2,1)}, u32[]{:S(2)}, u32[]{:S(2)}) async-start(bf16[64,4,3584]{2,1,0:T(4,128)(2,1)} %reshape.198), calls=%async_computation.3 | async-start | bytes 3670016 | tf_op jit(solution)/shard_map/all_to_all | solution.py:81
  216.0 2.8 copy-start.2
  216.0 2.8 copy-start.3
  216.0 89.5 %reduce-scatter.4.cloned.1.call-start = ((), (), s32[]{:S(2)}) async-start(), calls=%async_computation.5 | async-start | bytes 1032192
Sparse Core Ops, SparseCore 0:
  273.0 32.4 reduce-scatter.3
where the time goes:
time: 315 us; the launch traced here: 314 us
  waiting for transfers between devices  179 us (57%)
  local copies, waits for them, and re-layouts  48.6 us (15%)
  starting transfers between devices  39.8 us (13%)
  blocking collectives  15.1 us (5%)
  between operations  13.7 us (4%)
  matrix products  12.1 us (4%)
  other arithmetic  6 us (2%)
    all_to_all x2, waiting for transfers between devices, shards(): lax.all_to_all(batch, 'expert', split_axis=0, concat_axis=0, tiled=True)  76.8 us
    all_to_all x2, waiting for transfers between devices, shards(): lax.all_to_all(partial_value, 'expert', split_axis=0, concat_axis=0, tile...  69.4 us
    unnamed x2, waiting for transfers between devices  32.7 us
    all_to_all x2, starting transfers between devices, shards(): lax.all_to_all(batch, 'expert', split_axis=0, concat_axis=0, tiled=True)  25 us
    all_gather x1, blocking collectives, shards(): gathered = lax.all_gather(hidden_rows, 'tensor', axis=2, tiled=True)  15.1 us
    all_to_all x2, starting transfers between devices, shards(): lax.all_to_all(partial_value, 'expert', split_axis=0, concat_axis=0, tile...  14.8 us
    unnamed x21, local copies, waits for them, and re-layouts  13.6 us
    dot_general x2, matrix products, shards(): jnp.dot(hidden, slot_down[0], preferred_element_type=jnp.float32)  7.1 us
  transfers between devices with their start and end apart: 5, of which 5 were waited for; matrix products, arithmetic and copies ran while one was open for 12% of the time, Pallas kernels for 0%

commit v1 on v0

--- a/solution.py
+++ b/solution.py
@@ -45,7 +45,9 @@
     step_count, row_count, _ = hidden_rows.shape
     top_count = expert_ids.shape[2]
     capacity = row_count * top_count // (slot_count - slot_count // 8) + 2
-    gathered = lax.all_gather(hidden_rows, "tensor", axis=2, tiled=True)
+    gathered = jnp.concatenate(
+        lax.all_to_all(jnp.stack([hidden_rows] * lax.axis_size("tensor")), "tensor", 0, 0), axis=2
+    )
     width_full = gathered.shape[2]
     plans = [
         route_plan(

time: 315 us -> 297 us (0.943)
  blocking collectives: 15.1 us -> 0 us
  local copies, waits for them, and re-layouts: 48.6 us -> 40.9 us
  starting transfers between devices: 39.8 us -> 44.2 us
    all_gather x1 -> x0, blocking collectives: 15.1 us -> none  [shards(): gathered = lax.all_gather(hidden_rows, 'tensor', axis=2, tiled=True)]
    unnamed x21 -> x18, local copies, waits for them, and re-layouts: 13.6 us -> 7.39 us
    all_to_all x0 -> x1, starting transfers between devices: none -> 4.3 us  [shards(): lax.all_to_all(jnp.stack([hidden_rows] * lax.axis_size('tensor')), 'tenso...]
    slice x1 -> x3, local copies, waits for them, and re-layouts: 3.46 us -> 0.18 us  [shards(): source = gathered[index]]
    all_to_all x2, waiting for transfers between devices: 69.4 us -> 66.1 us  [shards(): lax.all_to_all(partial_value, 'expert', split_axis=0, concat_axis=0, tile...]
  transfers between devices with their start and end apart: 5 -> 6, of which waited for: 5 -> 6; matrix products, arithmetic and copies ran while one was open for 12% -> 13% of each run, Pallas kernels for 0% -> 0%
where the time goes in v1:
time: 297 us; the launch traced here: 296 us
  waiting for transfers between devices  179 us (60%)
  starting transfers between devices  44.2 us (15%)
  local copies, waits for them, and re-layouts  40.9 us (14%)
  between operations  13.7 us (5%)
  matrix products  12.1 us (4%)
  other arithmetic  6.01 us (2%)
    all_to_all x2, waiting for transfers between devices, shards(): lax.all_to_all(batch, 'expert', split_axis=0, concat_axis=0, tiled=True)  78.7 us
    all_to_all x2, waiting for transfers between devices, shards(): lax.all_to_all(partial_value, 'expert', split_axis=0, concat_axis=0, tile...  66.1 us
    unnamed x2, waiting for transfers between devices  32.4 us
    all_to_all x2, starting transfers between devices, shards(): lax.all_to_all(batch, 'expert', split_axis=0, concat_axis=0, tiled=True)  24.3 us
    all_to_all x2, starting transfers between devices, shards(): lax.all_to_all(partial_value, 'expert', split_axis=0, concat_axis=0, tile...  15.4 us
    unnamed x18, local copies, waits for them, and re-layouts  7.39 us
    dot_general x2, matrix products, shards(): jnp.dot(hidden, slot_down[0], preferred_element_type=jnp.float32)  7.1 us
  transfers between devices with their start and end apart: 6, of which 6 were waited for; matrix products, arithmetic and copies ran while one was open for 13% of the time, Pallas kernels for 0%

profile of v1, /device:TPU:8, one launch (start us, length us, event | category | flops | bytes accessed | tf_op | source)
XLA Modules:
  0.0 296.2 jit_solution(4271029169418685880)
XLA Ops:
  8.1 4.3 %all-to-all-start = ((bf16[8,2,16,448]{3,2,1,0:T(8,128)(2,1)}), bf16[8,2,16,448]{3,2,1,0:T(8,128)(2,1)S(1)}, u32[]{:S(2)}, u32[]{:S(2)}) async-start(bf16[8,2,16,448]{3,2,1,0:T(8,128)(2,1)} %stack.38), calls=%async_computation | async-start | bytes 524288 | tf_op jit(solution)/shard_map/all_to_all | solution.py:49
  17.9 2.0 all-to-all-done
  22.3 16.6 %all-to-all-start.3 = ((bf16[64,4,3584]{2,1,0:T(4,128)(2,1)}), bf16[64,4,3584]{2,1,0:T(4,128)(2,1)S(1)}, u32[]{:S(2)}, u32[]{:S(2)}) async-start(bf16[64,4,3584]{2,1,0:T(4,128)(2,1)} %reshape.207), calls=%async_computation.3 | async-start | bytes 3670016 | tf_op jit(solution)/shard_map/all_to_all | solution.py:74
  40.5 1.9 convolution_convert_fusion.3
  42.4 4.1 %reshape.202 = bf16[64,4,3584]{2,1,0:T(4,128)(2,1)} reshape(bf16[256,3584]{1,0:T(8,128)(2,1)} %convolution_convert_fusion.3) | data formatting | bytes 3670016 | tf_op jit(solution)/shard_map/reshape | solution.py:69
  46.5 38.8 %all-to-all-done.3 = bf16[64,4,3584]{2,1,0:T(4,128)(2,1)S(1)} async-done(((bf16[64,4,3584]{2,1,0:T(4,128)(2,1)}), bf16[64,4,3584]{2,1,0:T(4,128)(2,1)S(1)}, u32[]{:S(2)}, u32[]{:S(2)}) %all-to-all-start.3) | async-done | bytes 1835040 | tf_op jit(solution)/shard_map/all_to_all | solution.py:74
  85.3 7.7 %all-to-all-start.1 = ((bf16[64,4,3584]{2,1,0:T(4,128)(2,1)}), bf16[64,4,3584]{2,1,0:T(4,128)(2,1)}, u32[]{:S(2)}, u32[]{:S(2)}) async-start(bf16[64,4,3584]{2,1,0:T(4,128)(2,1)} %reshape.202), calls=%async_computation.1 | async-start | bytes 3670016 | tf_op jit(solution)/shard_map/all_to_all | solution.py:74
  94.5 2.9 convolution_convert_fusion
  98.9 39.9 %all-to-all-done.1 = bf16[64,4,3584]{2,1,0:T(4,128)(2,1)} async-done(((bf16[64,4,3584]{2,1,0:T(4,128)(2,1)}), bf16[64,4,3584]{2,1,0:T(4,128)(2,1)}, u32[]{:S(2)}, u32[]{:S(2)}) %all-to-all-start.1) | async-done | bytes 1835040 | tf_op jit(solution)/shard_map/all_to_all | solution.py:74
  138.7 7.6 %all-to-all-start.4 = ((bf16[64,4,3584]{2,1,0:T(4,128)(2,1)}), bf16[64,4,3584]{2,1,0:T(4,128)(2,1)S(1)}, u32[]{:S(2)}, u32[]{:S(2)}) async-start(bf16[64,4,3584]{2,1,0:T(4,128)(2,1)} %reshape.209), calls=%async_computation.4 | async-start | bytes 3670016 | tf_op jit(solution)/shard_map/all_to_all | solution.py:83
  146.4 3.9 %reshape.203 = bf16[256,3584]{1,0:T(8,128)(2,1)} reshape(bf16[64,4,3584]{2,1,0:T(4,128)(2,1)} %all-to-all-done.1) | data formatting | bytes 3670016 | tf_op jit(solution)/shard_map/reshape | solution.py:75
  150.3 4.2 %convolution_convert_fusion.1 = bf16[256,3584]{1,0:T(8,128)(2,1)} fusion(bf16[1,128,3584]{2,1,0:T(8,128)(2,1)S(1)} %copy-done, bf16[256,3584]{1,0:T(8,128)(2,1)} %reshape.203, bf16[1,3584,128]{2,1,0:T(8,128)(2,1)} %param.22), kind=kOutput, calls=%fused_computation.5 | convolution fusion | flops 470843392 | bytes 5505024 | tf_op jit(solution)/shard_map/dot_general | solution.py:79
  154.5 4.1 %reshape.204 = bf16[64,4,3584]{2,1,0:T(4,128)(2,1)} reshape(bf16[256,3584]{1,0:T(8,128)(2,1)} %convolution_convert_fusion.1) | data formatting | bytes 3670016 | tf_op jit(solution)/shard_map/reshape | solution.py:82
  158.5 31.5 %all-to-all-done.4 = bf16[64,4,3584]{2,1,0:T(4,128)(2,1)S(1)} async-done(((bf16[64,4,3584]{2,1,0:T(4,128)(2,1)}), bf16[64,4,3584]{2,1,0:T(4,128)(2,1)S(1)}, u32[]{:S(2)}, u32[]{:S(2)}) %all-to-all-start.4) | async-done | bytes 1835040 | tf_op jit(solution)/shard_map/all_to_all | solution.py:83
  191.3 7.8 %all-to-all-start.2 = ((bf16[64,4,3584]{2,1,0:T(4,128)(2,1)}), bf16[64,4,3584]{2,1,0:T(4,128)(2,1)}, u32[]{:S(2)}, u32[]{:S(2)}) async-start(bf16[64,4,3584]{2,1,0:T(4,128)(2,1)} %reshape.204), calls=%async_computation.2 | async-start | bytes 3670016 | tf_op jit(solution)/shard_map/all_to_all | solution.py:83
  202.5 3.0 reshape.210
  205.5 2.0 gather_fusion.3
  207.5 34.6 %all-to-all-done.2 = bf16[64,4,3584]{2,1,0:T(4,128)(2,1)} async-done(((bf16[64,4,3584]{2,1,0:T(4,128)(2,1)}), bf16[64,4,3584]{2,1,0:T(4,128)(2,1)}, u32[]{:S(2)}, u32[]{:S(2)}) %all-to-all-start.2) | async-done | bytes 1835040 | tf_op jit(solution)/shard_map/all_to_all | solution.py:83
  242.1 2.9 reshape.205
  245.1 2.0 gather_fusion.1
  247.1 1.9 bitcast_reduce_fusion
  249.0 1.9 bitcast_reduce_fusion.1
  251.1 2.4 copy.56
  255.2 32.4 %reduce-scatter.4.cloned.1.call-done = bf16[448,32]{1,0:T(8,128)(2,1)} async-done(((bf16[3584,32]{1,0:T(8,128)(2,1)}), bf16[448,32]{1,0:T(8,128)(2,1)}) %reduce-scatter.4.cloned.1.call-update) | async-done | bytes 28688
  (79 shorter events, 21.9 us)
Async XLA Ops:
  6.5 87.9 %copy-start = (bf16[1,128,3584]{2,1,0:T(8,128)(2,1)S(1)}, bf16[1,128,3584]{2,1,0:T(8,128)(2,1)}, u32[]{:S(2)}) copy-start(bf16[1,128,3584]{2,1,0:T(8,128)(2,1)} %param.23) | copy-start | bytes 2752516
  8.1 11.8 %all-to-all-start = ((bf16[8,2,16,448]{3,2,1,0:T(8,128)(2,1)}), bf16[8,2,16,448]{3,2,1,0:T(8,128)(2,1)S(1)}, u32[]{:S(2)}, u32[]{:S(2)}) async-start(bf16[8,2,16,448]{3,2,1,0:T(8,128)(2,1)} %stack.38), calls=%async_computation | async-start | bytes 524288 | tf_op jit(solution)/shard_map/all_to_all | solution.py:49
  22.3 62.9 %all-to-all-start.3 = ((bf16[64,4,3584]{2,1,0:T(4,128)(2,1)}), bf16[64,4,3584]{2,1,0:T(4,128)(2,1)S(1)}, u32[]{:S(2)}, u32[]{:S(2)}) async-start(bf16[64,4,3584]{2,1,0:T(4,128)(2,1)} %reshape.207), calls=%async_computation.3 | async-start | bytes 3670016 | tf_op jit(solution)/shard_map/all_to_all | solution.py:74
  85.3 53.5 %all-to-all-start.1 = ((bf16[64,4,3584]{2,1,0:T(4,128)(2,1)}), bf16[64,4,3584]{2,1,0:T(4,128)(2,1)}, u32[]{:S(2)}, u32[]{:S(2)}) async-start(bf16[64,4,3584]{2,1,0:T(4,128)(2,1)} %reshape.202), calls=%async_computation.1 | async-start | bytes 3670016 | tf_op jit(solution)/shard_map/all_to_all | solution.py:74
  138.7 51.3 %all-to-all-start.4 = ((bf16[64,4,3584]{2,1,0:T(4,128)(2,1)}), bf16[64,4,3584]{2,1,0:T(4,128)(2,1)S(1)}, u32[]{:S(2)}, u32[]{:S(2)}) async-start(bf16[64,4,3584]{2,1,0:T(4,128)(2,1)} %reshape.209), calls=%async_computation.4 | async-start | bytes 3670016 | tf_op jit(solution)/shard_map/all_to_all | solution.py:83
  158.5 40.8 %copy-start.4 = (f32[2,16,8]{1,2,0:T(8,128)S(1)}, f32[2,16,8]{1,2,0:T(8,128)}, u32[]{:S(2)}) copy-start(f32[2,16,8]{1,2,0:T(8,128)} %param.21) | copy-start | bytes 3076
  190.0 1.3 copy-start.1
  191.3 50.8 %all-to-all-start.2 = ((bf16[64,4,3584]{2,1,0:T(4,128)(2,1)}), bf16[64,4,3584]{2,1,0:T(4,128)(2,1)}, u32[]{:S(2)}, u32[]{:S(2)}) async-start(bf16[64,4,3584]{2,1,0:T(4,128)(2,1)} %reshape.204), calls=%async_computation.2 | async-start | bytes 3670016 | tf_op jit(solution)/shard_map/all_to_all | solution.py:83
  199.1 3.0 copy-start.2
  199.1 2.9 copy-start.3
  199.1 88.4 %reduce-scatter.4.cloned.1.call-start = ((), (), s32[]{:S(2)}) async-start(), calls=%async_computation.6 | async-start | bytes 1032192
Sparse Core Ops, SparseCore 0:
  255.3 32.2 reduce-scatter.3
